TPU v7x, 128 devices: a whole 4x4x4 slice. The times are simulated.
128 devices in a mesh: frames: 8 (over y, core), space: 16 (over x, z).
Axes of the slice: x: 4, y: 4, z: 4, core: 2. Of those that a mesh axis runs over, the one named last changes fastest.
Arguments:
- latent: bfloat16 [8, 32, 256, 1152], P('frames', 'space'), may hold values from -6 to 6
- query_rows: bfloat16 [8, 32, 256, 1152], P('frames', 'space'), may hold values from -5.5 to 5.5
- key_rows: bfloat16 [8, 32, 256, 1152], P('frames', 'space'), may hold values from -5.5 to 5.5
- value_rows: bfloat16 [8, 32, 256, 1152], P('frames', 'space'), may hold values from -6 to 6
- cached_out: bfloat16 [8, 32, 256, 1152], P('frames', 'space'), may hold values from -4 to 4
- refreshed: int32 [8, 32], P('frames', 'space'), may hold values from 0 to 1, as said below
- band_width: int32 [16], replicated, may hold values from 1 to 7, as said below
- out_weight: bfloat16 [1152, 1152], replicated, may hold values from -0.1875 to 0.1875
- temporal_weight: bfloat16 [1152, 3456], replicated, may hold values from -0.1360803 to 0.1360803
Outputs:
- mixed: bfloat16 [8, 32, 256, 1152], P('frames', 'space')
Inputs may be any that keep to these rules, and one draw needn't show every extreme that they name: `refreshed`: 1 marks a tile that is recomputed; tiles further down a frame are recomputed more often. `band_width`: at least one head reaches 7 frames.
All inputs are finite; a program needn't handle non-finite values.
Results may differ from a plain program's by a relative error of at most 0.008.
Values may be sent and summed in bfloat16 or wider, within the bound.
No kernel may reach another device: no remote copies, remote signals or barrier semaphores. Data moves between devices by JAX's collectives and lax.ppermute only.
A program may use at most 128 MiB of HBM per device.

v0:
```python
import math

import jax
import jax.numpy as jnp
from jax import lax
from jax.sharding import PartitionSpec as P

EDGE = 64


def shifted(block, axis, distance):
    devices = range(lax.axis_size(axis))
    route = [(i - distance, i) for i in devices if i - distance in devices]
    return lax.ppermute(block, axis, route)


def soft_rows(scores):
    top = jnp.max(scores, axis=-1, keepdims=True)
    expo = jnp.exp(scores - top)
    return expo / jnp.sum(expo, axis=-1, keepdims=True)


def attend(query_rows, key_ext, value_ext, usable, head_count):
    lead = query_rows.shape[:-2]
    tok_count, width = query_rows.shape[-2:]
    span = key_ext.shape[-2]
    head_dim = width // head_count
    scaling = 1.0 / math.sqrt(head_dim)
    query5 = query_rows.reshape(lead + (tok_count, head_count, head_dim))
    key5 = key_ext.reshape(lead + (span, head_count, head_dim))
    value5 = value_ext.reshape(lead + (span, head_count, head_dim))
    scores = (
        jnp.einsum("...qhe,...khe->...hqk", query5, key5, preferred_element_type=jnp.float32)
        * scaling
    )
    scores = jnp.where(usable[..., None, None, :], scores, -jnp.inf)
    weights = soft_rows(scores).astype(jnp.bfloat16)
    result = jnp.einsum(
        "...hqk,...khe->...qhe", weights, value5, preferred_element_type=jnp.float32
    )
    return result.astype(jnp.bfloat16).reshape(lead + (tok_count, width))


def temporal_block(block, band_width, head_count, width):
    adim, sdim, bdim, idim, pdim, _ = block.shape
    head_dim = width // head_count
    scaling = 1.0 / math.sqrt(head_dim)
    query6 = block[..., :width].reshape(adim, sdim, bdim, idim, pdim, head_count, head_dim)
    key6 = block[..., width : 2 * width].reshape(adim, sdim, bdim, idim, pdim, head_count, head_dim)
    value6 = block[..., 2 * width :].reshape(adim, sdim, bdim, idim, pdim, head_count, head_dim)
    scores = (
        jnp.einsum("asbiphe,csuiphe->siphabcu", query6, key6, preferred_element_type=jnp.float32)
        * scaling
    )
    frame_index = (
        jnp.arange(adim, dtype=jnp.int32)[:, None] * bdim
        + jnp.arange(bdim, dtype=jnp.int32)[None, :]
    )
    frame_gap = jnp.abs(frame_index[:, :, None, None] - frame_index[None, None, :, :])
    allowed = frame_gap[None] <= band_width[:, None, None, None, None]
    scores = jnp.where(allowed, scores, -jnp.inf)
    flat_scores = scores.reshape(sdim, idim, pdim, head_count, adim, bdim, adim * bdim)
    weights = soft_rows(flat_scores).astype(jnp.bfloat16)
    weights = weights.reshape(sdim, idim, pdim, head_count, adim, bdim, adim, bdim)
    result = jnp.einsum(
        "siphabcu,csuiphe->asbiphe", weights, value6, preferred_element_type=jnp.float32
    )
    return result.astype(jnp.bfloat16).reshape(adim * sdim * bdim, idim, pdim, width)


def local(
    latent,
    query_rows,
    key_rows,
    value_rows,
    cached_out,
    refreshed,
    band_width,
    out_weight,
    temporal_weight,
):
    frame_count, tile_count, tok_count, width = latent.shape
    head_count = band_width.shape[0]
    last_edges = jnp.stack([key_rows[:, -1, -EDGE:], value_rows[:, -1, -EDGE:]])
    first_edges = jnp.stack([key_rows[:, 0, :EDGE], value_rows[:, 0, :EDGE]])
    from_above = shifted(last_edges, "space", 1)
    from_below = shifted(first_edges, "space", -1)
    prev_key = jnp.concatenate([from_above[0][:, None], key_rows[:, :-1, -EDGE:]], axis=1)
    prev_value = jnp.concatenate([from_above[1][:, None], value_rows[:, :-1, -EDGE:]], axis=1)
    next_key = jnp.concatenate([key_rows[:, 1:, :EDGE], from_below[0][:, None]], axis=1)
    next_value = jnp.concatenate([value_rows[:, 1:, :EDGE], from_below[1][:, None]], axis=1)
    key_ext = jnp.concatenate([prev_key, key_rows, next_key], axis=2)
    value_ext = jnp.concatenate([prev_value, value_rows, next_value], axis=2)
    span = tok_count + 2 * EDGE
    total_tiles = tile_count * lax.axis_size("space")
    tile_index = (lax.axis_index("space") * tile_count + jnp.arange(tile_count, dtype=jnp.int32))[
        :, None
    ]
    position = jnp.arange(span, dtype=jnp.int32)[None, :]
    usable = ((position >= EDGE) | (tile_index > 0)) & (
        (position < EDGE + tok_count) | (tile_index < total_tiles - 1)
    )
    usable = usable[None]
    fresh = attend(query_rows, key_ext, value_ext, usable, head_count)
    spatial = jnp.where(refreshed[:, :, None, None] == 1, fresh, cached_out)
    projected = jnp.dot(spatial.reshape(-1, width), out_weight, preferred_element_type=jnp.float32)
    hidden = (latent.astype(jnp.float32) + projected.reshape(latent.shape)).astype(jnp.bfloat16)
    hidden32 = hidden.astype(jnp.float32)
    normed = (
        hidden32 * lax.rsqrt(jnp.mean(hidden32 * hidden32, axis=-1, keepdims=True) + 1e-06)
    ).astype(jnp.bfloat16)
    frame_groups = lax.axis_size("frames")
    space_groups = lax.axis_size("space")
    block = lax.all_to_all(normed, ("frames", "space"), split_axis=2, concat_axis=0, tiled=True)
    flat = jnp.dot(
        block.reshape(-1, width), temporal_weight, preferred_element_type=jnp.float32
    ).astype(jnp.bfloat16)
    wide_block = flat.reshape(block.shape[:-1] + (3 * width,))
    shaped = wide_block.reshape(
        frame_groups, space_groups, frame_count, wide_block.shape[1], wide_block.shape[2], 3 * width
    )
    attended = temporal_block(shaped, band_width, head_count, width)
    temporal = lax.all_to_all(
        attended, ("frames", "space"), split_axis=0, concat_axis=2, tiled=True
    )
    return (hidden32 + temporal.astype(jnp.float32)).astype(jnp.bfloat16)


def solution(mesh):
    return jax.shard_map(
        local,
        mesh=mesh,
        in_specs=(
            P("frames", "space", None, None),
            P("frames", "space", None, None),
            P("frames", "space", None, None),
            P("frames", "space", None, None),
            P("frames", "space", None, None),
            P("frames", "space"),
            P(),
            P(),
            P(),
        ),
        out_specs=P("frames", "space", None, None),
        check_vma=False,
    )
```

profile of v0, /device:TPU:6, one launch (start us, length us, event | category | flops | bytes accessed | tf_op | source)
XLA Modules:
  0.0 215.4 jit_solution(13134790568129760812)
XLA Ops:
  1.6 3.8 %collective-permute-start = (bf16[2,1,64,1152]{3,2,1,0:T(8,128)(2,1)S(1)}, bf16[2,1,64,1152]{3,2,1,0:T(8,128)(2,1)}, u32[]{:S(2)}, u32[]{:S(2)}) collective-permute-start(bf16[2,1,64,1152]{3,2,1,0:T(8,128)(2,1)S(1)} %pad_maximum_fusion), channel_id=1, source_target_pairs={{0,1},{1,2},{2,3},{3,4},{4,5},{5,6},{6,7},{7,8},{8,9},{9,10},{10,1... | collective-permute-start | bytes 884744 | tf_op jit(solution)/shard_map/ppermute | solution.py:14
  6.2 4.3 %collective-permute-start.1 = (bf16[2,1,64,1152]{3,2,1,0:T(8,128)(2,1)}, bf16[2,1,64,1152]{3,2,1,0:T(8,128)(2,1)}, u32[]{:S(2)}, u32[]{:S(2)}) collective-permute-start(bf16[2,1,64,1152]{3,2,1,0:T(8,128)(2,1)} %pad_maximum_fusion.1), channel_id=1, source_target_pairs={{1,0},{2,1},{3,2},{4,3},{5,4},{6,5},{7,6},{8,7},{9,8},{10,9},{11,1... | collective-permute-start | bytes 884744 | tf_op jit(solution)/shard_map/ppermute | solution.py:14
  10.5 2.4 %copy.33 = bf16[1,2,256,1152]{2,3,1,0:T(8,128)(2,1)} copy(bf16[1,2,256,1152]{3,2,1,0:T(8,128)(2,1)} %param.10) | data formatting | bytes 2359296 | tf_op args[1]
  18.1 2.7 %maximum_maximum_fusion.1 = bf16[1,2,384,1152]{3,2,1,0:T(8,128)(2,1)} fusion(bf16[1,1,64,1152]{3,2,1,0:T(8,128)(2,1)S(1)} %get-tuple-element.18, bf16[1,1,64,1152]{3,2,1,0:T(8,128)(2,1)S(1)} %get-tuple-element.11, bf16[1,2,256,1152]{3,2,1,0:T(8,128)(2,1)} %param.11, bf16[1,1,64,1152]{3,2,1,0:T(8,128)(2,1)S(1)} %get-tuple-element.8, ...), kind=kLoop, calls=%fused_computation.39 | loop fusion | flops 8847360 | bytes 3538944 | tf_op jit(solution)/shard_map/concatenate | solution.py:92
  20.7 3.9 %copy.32 = bf16[1,2,384,1152]{2,3,1,0:T(8,128)(2,1)} copy(bf16[1,2,384,1152]{3,2,1,0:T(8,128)(2,1)} %maximum_maximum_fusion.1) | data formatting | bytes 3538944 | tf_op jit(solution)/shard_map/concatenate | solution.py:92
  24.6 2.6 %maximum_maximum_fusion = bf16[1,2,384,1152]{3,2,1,0:T(8,128)(2,1)} fusion(bf16[1,1,64,1152]{3,2,1,0:T(8,128)(2,1)S(1)} %get-tuple-element.19, bf16[1,1,64,1152]{3,2,1,0:T(8,128)(2,1)S(1)} %get-tuple-element.28, bf16[1,2,256,1152]{3,2,1,0:T(8,128)(2,1)} %param.12, bf16[1,1,64,1152]{3,2,1,0:T(8,128)(2,1)S(1)} %get-tuple-element.27, ...), kind=kLoop, calls=%fused_computation.38 | loop fusion | flops 8847360 | bytes 3538944 | tf_op jit(solution)/shard_map/concatenate | solution.py:93
  27.2 3.9 %copy.31 = bf16[1,2,384,1152]{2,3,1,0:T(8,128)(2,1)} copy(bf16[1,2,384,1152]{3,2,1,0:T(8,128)(2,1)} %maximum_maximum_fusion) | data formatting | bytes 3538944 | tf_op jit(solution)/shard_map/concatenate | solution.py:93
  31.1 11.4 %fusion.45 = (f32[2,16,256]{2,1,0:T(8,128)S(1)}, f32[2,16,256,384]{2,3,1,0:T(8,128)}) fusion(pred[2,384]{1,0:T(4,128)(4,1)S(1)} %or_and_fusion, bf16[2,384,16,72]{1,3,2,0:T(8,128)(2,1)} %bitcast.71, bf16[2,256,16,72]{1,3,2,0:T(8,128)(2,1)} %bitcast.73), kind=kOutput, calls=%fused_computation.67 | convolution fusion | flops 465568128 | bytes 15565568 | tf_op jit(solution)/shard_map/sub | solution.py:19
  42.5 7.4 %fusion.28 = bf16[2,16,72,256]{3,2,1,0:T(8,128)(2,1)} fusion(bf16[2,384,16,72]{1,3,2,0:T(8,128)(2,1)} %bitcast.72, f32[2,16,256,384]{2,3,1,0:T(8,128)} %get-tuple-element.21, f32[2,16,256]{2,1,0:T(8,128)S(1)} %get-tuple-element.20), kind=kOutput, calls=%fused_computation.40 | convolution fusion | flops 459866112 | bytes 15564800 | tf_op jit(solution)/shard_map/...hqk,...khe->...qhe/dot_general | solution.py:38
  52.3 4.0 %fusion.14 = (f32[2,256]{1,0:T(2,128)S(1)}, bf16[1,2,256,1152]{3,2,1,0:T(8,128)(2,1)S(1)}) fusion(bf16[1152,1152]{1,0:T(8,128)(2,1)S(1)} %copy-done, bf16[1,2,256,1152]{3,2,1,0:T(8,128)(2,1)} %copy.35, bf16[1,2,256,1152]{3,2,1,0:T(8,128)(2,1)} %param.13, pred[2]{0:T(512)(128)(4,1)S(1)} %compare_bitcast_fusion, bf16[1,2,256,1152]{3,2,1,0:T(8,128)(2,1)} %param.9), kind=kOutput, calls=%fused_computation.24 | convolution fusion | flops 1363082752 | bytes 7374850 | tf_op jit(solution)/shard_map/dot_general | solution.py:106
  59.9 10.8 %all-to-all-start = ((bf16[1,2,256,1152]{3,1,0,2:T(2,128)(2,1)}), bf16[1,2,256,1152]{3,1,0,2:T(2,128)(2,1)S(1)}, u32[]{:S(2)}, u32[]{:S(2)}) async-start(bf16[1,2,256,1152]{3,1,0,2:T(2,128)(2,1)} %copy.36), calls=%async_computation | async-start | bytes 2359296 | tf_op jit(solution)/shard_map/all_to_all | solution.py:114
  70.7 18.3 %all-to-all-done = bf16[1,2,256,1152]{3,1,0,2:T(2,128)(2,1)S(1)} async-done(((bf16[1,2,256,1152]{3,1,0,2:T(2,128)(2,1)}), bf16[1,2,256,1152]{3,1,0,2:T(2,128)(2,1)S(1)}, u32[]{:S(2)}, u32[]{:S(2)}) %all-to-all-start) | async-done | bytes 1179680 | tf_op jit(solution)/shard_map/all_to_all | solution.py:114
  90.5 9.5 %convolution_convert_fusion = bf16[512,3456]{1,0:T(8,128)(2,1)} fusion(bf16[512,1152]{1,0:T(8,128)(2,1)S(1)} %reshape.243, bf16[1152,3456]{1,0:T(8,128)(2,1)} %param.17), kind=kOutput, calls=%fused_computation.12 | convolution fusion | flops 4078632960 | bytes 12681216 | tf_op jit(solution)/shard_map/dot_general | solution.py:115
  100.0 6.7 %reshape_reshape.3 = bf16[8,16,1,2,2,3456]{5,4,3,1,0,2:T(2,128)(2,1)S(1)} reshape(bf16[512,3456]{1,0:T(8,128)(2,1)} %convolution_convert_fusion) | data formatting | bytes 7077888 | tf_op jit(solution)/shard_map/reshape;reshape | solution.py:119
  106.7 3.5 %fusion.40 = (bf16[8,16,1,2,2,1152]{5,4,3,1,0,2:T(2,128)(2,1)}, bf16[8,16,1,2,2,1152]{5,4,3,1,0,2:T(2,128)(2,1)}, bf16[8,16,1,2,2,1152]{5,4,3,1,0,2:T(2,128)(2,1)}) fusion(bf16[8,16,1,2,2,3456]{5,4,3,1,0,2:T(2,128)(2,1)S(1)} %reshape_reshape.3), kind=kLoop, calls=%fused_computation.62 | loop fusion | bytes 7077888 | tf_op jit(solution)/shard_map/slice | solution.py:50
  110.2 5.9 %reshape.253 = bf16[8,16,2,2,16,72]{5,4,3,2,1,0:T(8,128)(2,1)S(1)} reshape(bf16[8,16,1,2,2,1152]{5,4,3,1,0,2:T(2,128)(2,1)} %get-tuple-element.6) | data formatting | bytes 2359296 | tf_op jit(solution)/shard_map/reshape.30
  116.1 6.6 %reshape.254 = bf16[8,16,2,2,16,72]{5,4,3,2,1,0:T(8,128)(2,1)} reshape(bf16[8,16,1,2,2,1152]{5,4,3,1,0,2:T(2,128)(2,1)} %get-tuple-element.7) | data formatting | bytes 2359296 | tf_op jit(solution)/shard_map/reshape.31
  122.7 5.3 %reshape.252 = bf16[8,16,2,2,16,72]{5,4,3,2,1,0:T(8,128)(2,1)} reshape(bf16[8,16,1,2,2,1152]{5,4,3,1,0,2:T(2,128)(2,1)S(1)} %copy-done.2) | data formatting | bytes 2359296 | tf_op jit(solution)/shard_map/reshape.35
  128.0 4.1 %fusion.18 = f32[16,2,2,16,8,8]{4,5,3,2,1,0:T(8,128)S(1)} fusion(bf16[8,16,2,2,16,72]{5,4,3,2,1,0:T(8,128)(2,1)} %reshape.254, bf16[8,16,2,2,16,72]{5,4,3,2,1,0:T(8,128)(2,1)S(1)} %reshape.253), kind=kOutput, calls=%fused_computation.29 | convolution fusion | flops 9437184 | bytes 2621440 | tf_op jit(solution)/shard_map/asbiphe,csuiphe->siphabcu/dot_general | solution.py:52
  132.1 41.7 %fusion.46 = (f32[16,2,2,16,8]{4,3,2,1,0:T(8,128)S(1)}, f32[16,2,2,16,8,8]{4,5,3,2,1,0:T(8,128)S(1)}) fusion(f32[16,2,2,16,8,8]{4,5,3,2,1,0:T(8,128)S(1)} %fusion.18, pred[16,8,8]{1,2,0:T(8,128)(4,1)S(1)} %broadcast_compare_fusion), kind=kOutput, calls=%fused_computation.68 | output fusion | flops 393223 | bytes 558080 | tf_op jit(solution)/shard_map/sub | solution.py:19
  176.3 4.4 %reshape.251 = bf16[128,2,2,1152]{3,2,1,0:T(2,128)(2,1)S(1)} reshape(bf16[8,16,1,2,2,16,72]{6,5,4,3,1,0,2:T(8,128)(2,1)S(1)} %copy.50) | data formatting | bytes 2359296 | tf_op jit(solution)/shard_map/reshape | solution.py:68
  180.7 24.4 %all_to_all.24 = bf16[128,2,2,1152]{3,2,1,0:T(2,128)(2,1)S(1)} all-to-all(bf16[128,2,2,1152]{3,2,1,0:T(2,128)(2,1)S(1)} %reshape.251), channel_id=1, replica_groups=mesh['frames'=8,'space'=16] {'frames','space'}, dimensions={0} | all-to-all | bytes 2359296 | tf_op jit(solution)/shard_map/all_to_all | solution.py:123
  208.1 4.2 %reshape.248 = f32[1,2,256,1152]{3,2,1,0:T(8,128)} reshape(f32[1,2,128,2,1152]{4,3,2,1,0:T(2,128)} %copy.47) | data formatting | bytes 4718592 | tf_op jit(solution)/shard_map/convert_element_type | solution.py:126
  212.2 3.2 %fusion.16 = bf16[1,2,256,1152]{3,2,1,0:T(8,128)(2,1)} fusion(f32[1,2,256,1152]{3,2,1,0:T(8,128)} %reshape.248, bf16[1,2,256,1152]{3,2,1,0:T(8,128)(2,1)} %copy-done.3), kind=kLoop, calls=%fused_computation.26 | loop fusion | flops 1769472 | bytes 4718592 | tf_op jit(solution)/shard_map/convert_element_type | solution.py:126
  (37 shorter events, 20.4 us)
Async XLA Ops:
  0.0 52.3 %copy-start = (bf16[1152,1152]{1,0:T(8,128)(2,1)S(1)}, bf16[1152,1152]{1,0:T(8,128)(2,1)}, u32[]{:S(2)}) copy-start(bf16[1152,1152]{1,0:T(8,128)(2,1)} %param.16) | copy-start | bytes 7962628
  1.6 11.3 %copy-start.6 = (s32[1,2]{1,0:T(1,128)S(1)}, s32[1,2]{1,0:T(1,128)}, u32[]{:S(2)}) copy-start(s32[1,2]{1,0:T(1,128)} %param.14) | copy-start | bytes 28
  1.6 13.3 %collective-permute-start = (bf16[2,1,64,1152]{3,2,1,0:T(8,128)(2,1)S(1)}, bf16[2,1,64,1152]{3,2,1,0:T(8,128)(2,1)}, u32[]{:S(2)}, u32[]{:S(2)}) collective-permute-start(bf16[2,1,64,1152]{3,2,1,0:T(8,128)(2,1)S(1)} %pad_maximum_fusion), channel_id=1, source_target_pairs={{0,1},{1,2},{2,3},{3,4},{4,5},{5,6},{6,7},{7,8},{8,9},{9,10},{10,1... | collective-permute-start | bytes 884744 | tf_op jit(solution)/shard_map/ppermute | solution.py:14
  6.2 10.9 %collective-permute-start.1 = (bf16[2,1,64,1152]{3,2,1,0:T(8,128)(2,1)}, bf16[2,1,64,1152]{3,2,1,0:T(8,128)(2,1)}, u32[]{:S(2)}, u32[]{:S(2)}) collective-permute-start(bf16[2,1,64,1152]{3,2,1,0:T(8,128)(2,1)} %pad_maximum_fusion.1), channel_id=1, source_target_pairs={{1,0},{2,1},{3,2},{4,3},{5,4},{6,5},{7,6},{8,7},{9,8},{10,9},{11,1... | collective-permute-start | bytes 884744 | tf_op jit(solution)/shard_map/ppermute | solution.py:14
  56.3 1.1 copy-start.3
  57.6 13.0 %copy-start.5 = (s32[16]{0:T(128)S(1)}, s32[16]{0:T(128)}, u32[]{:S(2)}) copy-start(s32[16]{0:T(128)} %param.15) | copy-start | bytes 196
  59.9 29.2 %all-to-all-start = ((bf16[1,2,256,1152]{3,1,0,2:T(2,128)(2,1)}), bf16[1,2,256,1152]{3,1,0,2:T(2,128)(2,1)S(1)}, u32[]{:S(2)}, u32[]{:S(2)}) async-start(bf16[1,2,256,1152]{3,1,0,2:T(2,128)(2,1)} %copy.36), calls=%async_computation | async-start | bytes 2359296 | tf_op jit(solution)/shard_map/all_to_all | solution.py:114
  116.1 6.6 %copy-start.2 = (bf16[8,16,1,2,2,1152]{5,4,3,1,0,2:T(2,128)(2,1)S(1)}, bf16[8,16,1,2,2,1152]{5,4,3,1,0,2:T(2,128)(2,1)}, u32[]{:S(2)}) copy-start(bf16[8,16,1,2,2,1152]{5,4,3,1,0,2:T(2,128)(2,1)} %get-tuple-element.5) | copy-start | bytes 3538948
  132.1 41.8 %copy-start.4 = (bf16[8,16,2,2,16,72]{5,4,3,2,1,0:T(8,128)(2,1)S(1)}, bf16[8,16,2,2,16,72]{5,4,3,2,1,0:T(8,128)(2,1)}, u32[]{:S(2)}) copy-start(bf16[8,16,2,2,16,72]{5,4,3,2,1,0:T(8,128)(2,1)} %reshape.252) | copy-start | bytes 3538948
  208.1 7.4 %copy-start.1 = (bf16[1152,1152]{1,0:T(8,128)(2,1)S(1)}, bf16[1152,1152]{1,0:T(8,128)(2,1)}, u32[]{:S(2)}) copy-start(bf16[1152,1152]{1,0:T(8,128)(2,1)} %param.16) | copy-start | bytes 7962628
where the time goes:
time: 219 us; the launch traced here: 215 us
  local copies, waits for them, and re-layouts  60.1 us (27%)
  other arithmetic  52.3 us (24%)
  matrix products  38.3 us (17%)
  blocking collectives  24.4 us (11%)
  waiting for transfers between devices  21.3 us (10%)
  starting transfers between devices  18.9 us (9%)
    sub x1, other arithmetic, soft_rows(): expo = jnp.exp(scores - top)  41.7 us
    all_to_all x1, blocking collectives, local(): lax.all_to_all(attended, ('frames', 'space'), split_axis=0, concat_axis=2...  24.4 us
    all_to_all x1, waiting for transfers between devices, local(): lax.all_to_all(normed, ('frames', 'space'), split_axis=2, concat_axis=0,...  18.3 us
    another operation x3, local copies, waits for them, and re-layouts  17.8 us
    sub x1, matrix products, soft_rows(): expo = jnp.exp(scores - top)  11.4 us
    all_to_all x1, starting transfers between devices, local(): lax.all_to_all(normed, ('frames', 'space'), split_axis=2, concat_axis=0,...  10.8 us
    dot_general x1, matrix products, local(): jnp.dot(block.reshape(-1, width), temporal_weight, preferred_element_type...  9.54 us
    ppermute x2, starting transfers between devices, shifted(): return lax.ppermute(block, axis, route)  8.12 us
  transfers between devices with their start and end apart: 3, of which 3 were waited for; matrix products, arithmetic and copies ran while one was open for 2% of the time, Pallas kernels for 0%

commit v1 on v0

v1 whole, which is shorter than its diff:
```python
import functools
import math

import jax
import jax.numpy as jnp
from jax import lax
from jax.experimental import pallas as pl
from jax.experimental.pallas import tpu as pltpu
from jax.sharding import PartitionSpec as P

EDGE = 64
HEADS = 16


def shifted(block, axis, distance):
    devices = range(lax.axis_size(axis))
    route = [(i - distance, i) for i in devices if i - distance in devices]
    return lax.ppermute(block, axis, route)


def head_window(h, head_dim, width):
    lo = h * head_dim
    start = min((lo // 128) * 128, width - 256)
    return lo, start


def spatial_kernel(flags_ref, q_ref, k_ref, v_ref, kp_ref, kn_ref, vp_ref, vn_ref,
                   lat_ref, cache_ref, wo_ref, hid_ref, nrm_ref, acc_ref, sp_ref):
    i = pl.program_id(0)
    refreshed = flags_ref[i, 0]
    prev_ok = flags_ref[i, 1] == 1
    next_ok = flags_ref[i, 2] == 1
    width = q_ref.shape[-1]
    head_dim = width // HEADS
    scaling = 1.0 / math.sqrt(head_dim)
    nt = (((1,), (1,)), ((), ()))

    @pl.when(refreshed == 1)
    def _():
        acc_ref[...] = jnp.zeros_like(acc_ref)
        for h in range(HEADS):
            lo, start = head_window(h, head_dim, width)
            win = pl.ds(start, 256)
            lane = lax.broadcasted_iota(jnp.int32, (1, 256), 1) + start
            mask = (lane >= lo) & (lane < lo + head_dim)
            qh = jnp.where(mask, q_ref[0, :, win], jnp.zeros((), q_ref.dtype))
            s_mid = lax.dot_general(qh, k_ref[0, :, win], nt,
                                    preferred_element_type=jnp.float32) * scaling
            s_prev = lax.dot_general(qh, kp_ref[0, :, win], nt,
                                     preferred_element_type=jnp.float32) * scaling
            s_next = lax.dot_general(qh, kn_ref[0, :, win], nt,
                                     preferred_element_type=jnp.float32) * scaling
            s_prev = jnp.where(prev_ok, s_prev, -jnp.inf)
            s_next = jnp.where(next_ok, s_next, -jnp.inf)
            top = jnp.maximum(
                jnp.maximum(jnp.max(s_mid, axis=1, keepdims=True),
                            jnp.max(s_prev, axis=1, keepdims=True)),
                jnp.max(s_next, axis=1, keepdims=True))
            e_mid = jnp.exp(s_mid - top)
            e_prev = jnp.exp(s_prev - top)
            e_next = jnp.exp(s_next - top)
            total = (jnp.sum(e_mid, axis=1, keepdims=True)
                     + jnp.sum(e_prev, axis=1, keepdims=True)
                     + jnp.sum(e_next, axis=1, keepdims=True))
            p_mid = (e_mid / total).astype(jnp.bfloat16)
            p_prev = (e_prev / total).astype(jnp.bfloat16)
            p_next = (e_next / total).astype(jnp.bfloat16)
            out = jnp.dot(p_mid, v_ref[0, :, win], preferred_element_type=jnp.float32)
            out = out + jnp.dot(p_prev, vp_ref[0, :, win], preferred_element_type=jnp.float32)
            out = out + jnp.dot(p_next, vn_ref[0, :, win], preferred_element_type=jnp.float32)
            acc_ref[:, win] += jnp.where(mask, out, 0.0)
        sp_ref[...] = acc_ref[...].astype(sp_ref.dtype)

    @pl.when(refreshed != 1)
    def _():
        sp_ref[...] = cache_ref[0]

    projected = jnp.dot(sp_ref[...], wo_ref[...], preferred_element_type=jnp.float32)
    hidden = (lat_ref[0].astype(jnp.float32) + projected).astype(jnp.bfloat16)
    hid_ref[0] = hidden
    h32 = hidden.astype(jnp.float32)
    ms = jnp.mean(h32 * h32, axis=-1, keepdims=True)
    nrm_ref[0] = (h32 * lax.rsqrt(ms + 1e-06)).astype(nrm_ref.dtype)


def spatial_block(flags, q, k, v, kp, kn, vp, vn, lat, cache, wo):
    tiles, tok, width = q.shape
    tile_spec = pl.BlockSpec((1, tok, width), lambda i, f: (i, 0, 0))
    edge_spec = pl.BlockSpec((1, EDGE, width), lambda i, f: (i, 0, 0))
    w_spec = pl.BlockSpec((width, width), lambda i, f: (0, 0))
    out_shape = [jax.ShapeDtypeStruct((tiles, tok, width), jnp.bfloat16)] * 2
    flops = tiles * (HEADS * 4 * tok * (tok + 2 * EDGE) * 256 + 2 * tok * width * width)
    cost = pl.CostEstimate(flops=flops, transcendentals=tiles * HEADS * tok * (tok + 2 * EDGE),
                           bytes_accessed=2 * (7 * tiles * tok * width + width * width))
    return pl.pallas_call(
        spatial_kernel,
        grid_spec=pltpu.PrefetchScalarGridSpec(
            num_scalar_prefetch=1,
            grid=(tiles,),
            in_specs=[tile_spec] * 3 + [edge_spec] * 4 + [tile_spec] * 2 + [w_spec],
            out_specs=[tile_spec, tile_spec],
            scratch_shapes=[pltpu.VMEM((tok, width), jnp.float32),
                            pltpu.VMEM((tok, width), jnp.bfloat16)],
        ),
        out_shape=out_shape,
        compiler_params=pltpu.CompilerParams(dimension_semantics=("arbitrary",),
                                             vmem_limit_bytes=48 * 1024 * 1024),
        cost_estimate=cost,
    )(flags, q, k, v, kp, kn, vp, vn, lat, cache, wo)


def temporal_kernel(bw_ref, q_ref, k_ref, v_ref, ind_ref, indt_ref, o_ref):
    frames, tok, width = q_ref.shape
    head_dim = width // HEADS
    scaling = 1.0 / math.sqrt(head_dim)
    bw = bw_ref[...]
    ind = ind_ref[...]
    indt = indt_ref[...]

    def body(f, carry):
        qf = q_ref[f].astype(jnp.float32)
        scores = []
        for g in range(frames):
            prod = qf * k_ref[g].astype(jnp.float32)
            s = jnp.dot(prod, ind, preferred_element_type=jnp.float32,
                        precision=lax.Precision.HIGHEST) * scaling
            allowed = jnp.abs(f - g) <= bw
            scores.append(jnp.where(allowed, s, -jnp.inf))
        top = scores[0]
        for s in scores[1:]:
            top = jnp.maximum(top, s)
        expo = [jnp.exp(s - top) for s in scores]
        total = expo[0]
        for e in expo[1:]:
            total = total + e
        out = jnp.zeros((tok, width), jnp.float32)
        for g in range(frames):
            p = (expo[g] / total).astype(jnp.bfloat16)
            wide = jnp.dot(p, indt, preferred_element_type=jnp.float32)
            out = out + wide * v_ref[g].astype(jnp.float32)
        o_ref[f] = out.astype(o_ref.dtype)
        return carry

    lax.fori_loop(0, frames, body, 0)


def temporal_attend(packed, band_width):
    frames, tok, wide = packed.shape
    width = wide // 3
    q = packed[..., :width]
    k = packed[..., width:2 * width]
    v = packed[..., 2 * width:]
    head_dim = width // HEADS
    ind = (jnp.arange(width, dtype=jnp.int32)[:, None] // head_dim
           == jnp.arange(HEADS, dtype=jnp.int32)[None, :])
    vspec = pl.BlockSpec(memory_space=pltpu.VMEM)
    cost = pl.CostEstimate(flops=frames * frames * tok * width * 40,
                           transcendentals=frames * frames * tok * HEADS,
                           bytes_accessed=2 * 4 * frames * tok * width)
    return pl.pallas_call(
        temporal_kernel,
        in_specs=[vspec] * 6,
        out_specs=vspec,
        out_shape=jax.ShapeDtypeStruct((frames, tok, width), jnp.bfloat16),
        compiler_params=pltpu.CompilerParams(vmem_limit_bytes=48 * 1024 * 1024),
        cost_estimate=cost,
    )(band_width.reshape(1, HEADS), q, k, v, ind.astype(jnp.float32),
      ind.T.astype(jnp.bfloat16))


def local(latent, query_rows, key_rows, value_rows, cached_out, refreshed, band_width,
          out_weight, temporal_weight):
    _, tile_count, tok_count, width = latent.shape
    lat = latent[0]
    q = query_rows[0]
    k = key_rows[0]
    v = value_rows[0]
    cache = cached_out[0]
    last_edges = jnp.stack([k[-1, -EDGE:], v[-1, -EDGE:]])
    first_edges = jnp.stack([k[0, :EDGE], v[0, :EDGE]])
    from_above = shifted(last_edges, "space", 1)
    from_below = shifted(first_edges, "space", -1)
    kp = jnp.concatenate([from_above[0][None], k[:-1, -EDGE:]], axis=0)
    vp = jnp.concatenate([from_above[1][None], v[:-1, -EDGE:]], axis=0)
    kn = jnp.concatenate([k[1:, :EDGE], from_below[0][None]], axis=0)
    vn = jnp.concatenate([v[1:, :EDGE], from_below[1][None]], axis=0)
    total_tiles = tile_count * lax.axis_size("space")
    tile_index = lax.axis_index("space") * tile_count + jnp.arange(tile_count, dtype=jnp.int32)
    flags = jnp.stack([refreshed[0].astype(jnp.int32),
                       (tile_index > 0).astype(jnp.int32),
                       (tile_index < total_tiles - 1).astype(jnp.int32)], axis=1)
    hidden, normed = spatial_block(flags, q, k, v, kp, kn, vp, vn, lat, cache, out_weight)

    frame_groups = lax.axis_size("frames")
    block = lax.all_to_all(normed[None], "frames", split_axis=2, concat_axis=0, tiled=True)
    rows = block.shape[1] * block.shape[2]
    flat = jnp.dot(block.reshape(-1, width), temporal_weight,
                   preferred_element_type=jnp.float32).astype(jnp.bfloat16)
    packed = flat.reshape(frame_groups, rows, 3 * width)
    attended = temporal_attend(packed, band_width)
    attended = attended.reshape(frame_groups, tile_count, -1, width)
    temporal = lax.all_to_all(attended, "frames", split_axis=0, concat_axis=2, tiled=True)
    mixed = (hidden.astype(jnp.float32) + temporal[0].astype(jnp.float32)).astype(jnp.bfloat16)
    return mixed[None]


def solution(mesh):
    return jax.shard_map(
        local,
        mesh=mesh,
        in_specs=(
            P("frames", "space", None, None),
            P("frames", "space", None, None),
            P("frames", "space", None, None),
            P("frames", "space", None, None),
            P("frames", "space", None, None),
            P("frames", "space"),
            P(),
            P(),
            P(),
        ),
        out_specs=P("frames", "space", None, None),
        check_vma=False,
    )
```

time: 219 us -> 115 us (0.53); the launches traced: 215 us -> 114 us
  local copies, waits for them, and re-layouts: 60.1 us -> 4.86 us
  other arithmetic: 52.3 us -> 2.07 us
  matrix products: 38.3 us -> 8.42 us
  Pallas kernels: 0 us -> 28.1 us
  waiting for transfers between devices: 21.3 us -> 27.3 us
  starting transfers between devices: 18.9 us -> 23.6 us
  blocking collectives: 24.4 us -> 19.8 us
    sub x1 -> x0, other arithmetic: 41.7 us -> none  [soft_rows(): expo = jnp.exp(scores - top)]
    pallas_call x0 -> x2, Pallas kernels: none -> 28.1 us  [the longest x1 22.6 us: temporal_attend(): pl.pallas_call(temporal_kernel, in_specs=[vspec] * 6, out_specs=vspec, ou...]
    another operation x4 -> x1, local copies, waits for them, and re-layouts: 24.5 us -> 0.09 us  [local(): jnp.stack([refreshed[0].astype(jnp.int32), (tile_index > 0).astype(jnp.in...]
    dot_general x4 -> x0, matrix products: 17.4 us -> none  [the longest x1 7.44 us: attend(): jnp.einsum('...hqk,...khe->...qhe', weights, value5, preferred_element_ty...]
    sub x1 -> x0, matrix products: 11.4 us -> none  [soft_rows(): expo = jnp.exp(scores - top)]
    convert_element_type x3 -> x1, local copies, waits for them, and re-layouts: 8.62 us -> 0.16 us  [local(): temporal[0].astype(jnp.float32)]
    reshape x4 -> x0, local copies, waits for them, and re-layouts: 7.8 us -> none  [the longest x2 4.94 us: temporal_block(): result.astype(jnp.bfloat16).reshape(adim * sdim * bdim, idim, pdim, width)]
    concatenate x2 -> x0, local copies, waits for them, and re-layouts: 7.71 us -> none  [the longest x1 3.86 us: local(): value_ext = jnp.concatenate([prev_value, value_rows, next_value], axis=2)]
  transfers between devices with their start and end apart: 3 -> 3, of which waited for: 3 -> 3; matrix products, arithmetic and copies ran while one was open for 2% -> 0% of each run, Pallas kernels for 0% -> 0%
where the time goes in v1:
time: 115 us; the launch traced here: 114 us
  Pallas kernels  28.1 us (24%)
  waiting for transfers between devices  27.3 us (24%)
  starting transfers between devices  23.6 us (21%)
  blocking collectives  19.8 us (17%)
  matrix products  8.42 us (7%)
  local copies, waits for them, and re-layouts  4.86 us (4%)
  other arithmetic  2.07 us (2%)
    pallas_call x1, Pallas kernels, temporal_attend(): pl.pallas_call(temporal_kernel, in_specs=[vspec] * 6, out_specs=vspec, ou...  22.6 us
    all_to_all x1, blocking collectives, local(): lax.all_to_all(attended, 'frames', split_axis=0, concat_axis=2, tiled=True)  19.8 us
    all_to_all x1, waiting for transfers between devices, local(): lax.all_to_all(normed[None], 'frames', split_axis=2, concat_axis=0, tiled...  17.1 us
    all_to_all x1, starting transfers between devices, local(): lax.all_to_all(normed[None], 'frames', split_axis=2, concat_axis=0, tiled...  15.5 us
    ppermute x2, waiting for transfers between devices, shifted(): return lax.ppermute(block, axis, route)  10.2 us
    dot_general x1, matrix products, local(): jnp.dot(block.reshape(-1, width), temporal_weight, preferred_element_type...  8.42 us
    ppermute x2, starting transfers between devices, shifted(): return lax.ppermute(block, axis, route)  8.13 us
    pallas_call x1, Pallas kernels, spatial_block(): pl.pallas_call(spatial_kernel, grid_spec=pltpu.PrefetchScalarGridSpec(num...  5.58 us
  transfers between devices with their start and end apart: 3, of which 3 were waited for; matrix products, arithmetic and copies ran while one was open for 0% of the time, Pallas kernels for 0%

profile of v1, /device:TPU:6, one launch (start us, length us, event | category | flops | bytes accessed | tf_op | source)
XLA Modules:
  0.0 114.4 jit_solution(4432827943047272960)
XLA Ops:
  0.0 1.4 %fusion.7 = (bf16[1,64,1152]{2,1,0:T(8,128)(2,1)S(1)}, bf16[1,64,1152]{2,1,0:T(8,128)(2,1)S(1)}, bf16[1,64,1152]{2,1,0:T(8,128)(2,1)S(1)}, bf16[1,64,1152]{2,1,0...) fusion(bf16[2,256,1152]{2,1,0:T(8,128)(2,1)} %bitcast.34, ...), kind=kLoop, calls=%fused_computation.26 | loop fusion | bytes 2359296 | tf_op jit(solution)/shard_map/slice | solution.py:186
  1.5 6.2 %collective-permute-start.1 = (bf16[2,64,1152]{2,1,0:T(8,128)(2,1)S(1)}, bf16[2,64,1152]{2,1,0:T(8,128)(2,1)S(1)}, u32[]{:S(2)}, u32[]{:S(2)}) collective-permute-start(bf16[2,64,1152]{2,1,0:T(8,128)(2,1)S(1)} %pad_maximum_fusion.2), channel_id=1, source_target_pairs={{1,0},{2,1},{3,2},{4,3},{5,4},{6,5},{7,6},{8,7},{9,8},{10,9},{11,1... | collective-permute-start | bytes 884744 | tf_op jit(solution)/shard_map/ppermute | solution.py:18
  7.8 1.9 %collective-permute-start = (bf16[2,64,1152]{2,1,0:T(8,128)(2,1)S(1)}, bf16[2,64,1152]{2,1,0:T(8,128)(2,1)S(1)}, u32[]{:S(2)}, u32[]{:S(2)}) collective-permute-start(bf16[2,64,1152]{2,1,0:T(8,128)(2,1)S(1)} %pad_maximum_fusion), channel_id=1, source_target_pairs={{0,1},{1,2},{2,3},{3,4},{4,5},{5,6},{6,7},{7,8},{8,9},{9,10},{10,1... | collective-permute-start | bytes 884744 | tf_op jit(solution)/shard_map/ppermute | solution.py:18
  9.7 0.1 copy.18
  9.8 0.1 pad_add_fusion.flags_ref
  9.9 4.1 %collective-permute-done.1 = bf16[2,64,1152]{2,1,0:T(8,128)(2,1)S(1)} collective-permute-done((bf16[2,64,1152]{2,1,0:T(8,128)(2,1)S(1)}, bf16[2,64,1152]{2,1,0:T(8,128)(2,1)S(1)}, u32[]{:S(2)}, u32[]{:S(2)}) %collective-permute-start.1) | collective-permute-done | bytes 294944 | tf_op jit(solution)/shard_map/ppermute | solution.py:18
  14.0 0.0 copy-start.2
  14.1 6.1 %collective-permute-done = bf16[2,64,1152]{2,1,0:T(8,128)(2,1)S(1)} collective-permute-done((bf16[2,64,1152]{2,1,0:T(8,128)(2,1)S(1)}, bf16[2,64,1152]{2,1,0:T(8,128)(2,1)S(1)}, u32[]{:S(2)}, u32[]{:S(2)}) %collective-permute-start) | collective-permute-done | bytes 294944 | tf_op jit(solution)/shard_map/ppermute | solution.py:18
  20.4 5.6 %shard_map.91 = (bf16[2,256,1152]{2,1,0:T(8,128)(2,1)S(1)}, bf16[2,256,1152]{2,1,0:T(8,128)(2,1)S(1)}) custom-call(s32[2,3]{1,0:T(2,128)S(1)} %pad_add_fusion.flags_ref, bf16[2,256,1152]{2,1,0:T(8,128)(2,1)S(1)} %bitcast.29, bf16[2,256,1152]{2,1,0:T(8,128)(2,1)S(1)} %bitcast.27, bf16[2,256,1152]{2,1,0:T(8,128)(2,1)} %bitcast.35, ...), custom_call_target="tpu_custom_call" | custom-call | flops 4580179968 | bytes 10911744 | tf_op jit(solution)/shard_map/pallas_call | solution.py:95
  25.9 2.2 %copy.19 = bf16[1,2,256,1152]{3,1,0,2:T(2,128)(2,1)} copy(bf16[1,2,256,1152]{3,2,1,0:T(8,128)(2,1)S(1)} %bitcast.25) | data formatting | bytes 2359296 | tf_op jit(solution)/shard_map/broadcast_in_dim | solution.py:195
  28.2 15.5 %all-to-all-start = ((bf16[1,2,256,1152]{3,1,0,2:T(2,128)(2,1)}), bf16[1,2,256,1152]{3,1,0,2:T(2,128)(2,1)S(1)}, u32[]{:S(2)}, u32[]{:S(2)}) async-start(bf16[1,2,256,1152]{3,1,0,2:T(2,128)(2,1)} %copy.19), calls=%async_computation | async-start | bytes 2359296 | tf_op jit(solution)/shard_map/all_to_all | solution.py:195
  43.7 0.2 fusion.1.ind_ref
  43.9 17.1 %all-to-all-done = bf16[1,2,256,1152]{3,1,0,2:T(2,128)(2,1)S(1)} async-done(((bf16[1,2,256,1152]{3,1,0,2:T(2,128)(2,1)}), bf16[1,2,256,1152]{3,1,0,2:T(2,128)(2,1)S(1)}, u32[]{:S(2)}, u32[]{:S(2)}) %all-to-all-start) | async-done | bytes 1179680 | tf_op jit(solution)/shard_map/all_to_all | solution.py:195
  61.0 0.1 copy.20
  61.1 0.1 copy.21
  61.2 8.4 %convolution_convert_fusion = bf16[512,3456]{1,0:T(8,128)(2,1)S(1)} fusion(bf16[512,1152]{1,0:T(8,128)(2,1)S(1)} %bitcast.33, bf16[1152,3456]{1,0:T(8,128)(2,1)} %param.17), kind=kOutput, calls=%fused_computation | convolution fusion | flops 4078632960 | bytes 12681216 | tf_op jit(solution)/shard_map/dot_general | solution.py:197
  69.7 0.0 copy-start.1
  69.7 0.5 fusion.6
  70.2 0.1 copy-done.1
  70.3 22.6 %shard_map.92 = bf16[8,64,1152]{2,1,0:T(8,128)(2,1)S(1)} custom-call(s32[1,16]{1,0:T(1,128)S(1)} %bitcast.28, bf16[8,64,1152]{2,1,0:T(8,128)(2,1)S(1)} %get-tuple-element.11.q_ref, bf16[8,64,1152]{2,1,0:T(8,128)(2,1)S(1)} %get-tuple-element.10.k_ref, bf16[8,64,1152]{2,1,0:T(8,128)(2,1)S(1)} %get-tuple-element.9.v_ref, f32[1152,16]{1,0:T(8,128)S(1)} %fusion.1.ind_ref, ...), custom_call_target="tpu_custom_call" | custom-call | flops 188743680 | bytes 4718592 | tf_op jit(solution)/shard_map/pallas_call | solution.py:160
  92.9 19.8 %all_to_all.24 = bf16[8,2,32,1152]{3,2,1,0:T(8,128)(2,1)S(1)} all-to-all(bf16[8,2,32,1152]{3,2,1,0:T(8,128)(2,1)S(1)} %bitcast.24), channel_id=1, replica_groups=mesh['frames'=8,'space'=16] {'frames'}, dimensions={0} | all-to-all | bytes 2359296 | tf_op jit(solution)/shard_map/all_to_all | solution.py:202
  112.7 0.2 convert_bitcast_fusion
  112.9 0.2 copy.22
  113.1 1.3 %fusion = bf16[1,2,256,1152]{3,2,1,0:T(8,128)(2,1)} fusion(f32[2,256,1152]{2,1,0:T(8,128)S(1)} %bitcast.30, bf16[2,256,1152]{2,1,0:T(8,128)(2,1)S(1)} %get-tuple-element.7), kind=kLoop, calls=%fused_computation.3 | loop fusion | flops 1769472 | bytes 4718592 | tf_op jit(solution)/shard_map/broadcast_in_dim | solution.py:204
  (16 shorter events, 0.3 us)
Async XLA Ops:
  1.4 8.2 %copy-start.3 = (s32[1,2]{1,0:T(1,128)S(1)}, s32[1,2]{1,0:T(1,128)}, u32[]{:S(2)}) copy-start(s32[1,2]{1,0:T(1,128)} %param.14) | copy-start | bytes 28
  1.5 12.5 %collective-permute-start.1 = (bf16[2,64,1152]{2,1,0:T(8,128)(2,1)S(1)}, bf16[2,64,1152]{2,1,0:T(8,128)(2,1)S(1)}, u32[]{:S(2)}, u32[]{:S(2)}) collective-permute-start(bf16[2,64,1152]{2,1,0:T(8,128)(2,1)S(1)} %pad_maximum_fusion.2), channel_id=1, source_target_pairs={{1,0},{2,1},{3,2},{4,3},{5,4},{6,5},{7,6},{8,7},{9,8},{10,9},{11,1... | collective-permute-start | bytes 884744 | tf_op jit(solution)/shard_map/ppermute | solution.py:18
  7.8 12.5 %collective-permute-start = (bf16[2,64,1152]{2,1,0:T(8,128)(2,1)S(1)}, bf16[2,64,1152]{2,1,0:T(8,128)(2,1)S(1)}, u32[]{:S(2)}, u32[]{:S(2)}) collective-permute-start(bf16[2,64,1152]{2,1,0:T(8,128)(2,1)S(1)} %pad_maximum_fusion), channel_id=1, source_target_pairs={{0,1},{1,2},{2,3},{3,4},{4,5},{5,6},{6,7},{7,8},{8,9},{9,10},{10,1... | collective-permute-start | bytes 884744 | tf_op jit(solution)/shard_map/ppermute | solution.py:18
  14.0 6.3 %copy-start = (bf16[1,2,256,1152]{3,2,1,0:T(8,128)(2,1)S(1)}, bf16[1,2,256,1152]{3,2,1,0:T(8,128)(2,1)}, u32[]{:S(2)}) copy-start(bf16[1,2,256,1152]{3,2,1,0:T(8,128)(2,1)} %param.11) | copy-start | bytes 3538948
  14.0 6.3 %copy-start.2 = (bf16[1,2,256,1152]{3,2,1,0:T(8,128)(2,1)S(1)}, bf16[1,2,256,1152]{3,2,1,0:T(8,128)(2,1)}, u32[]{:S(2)}) copy-start(bf16[1,2,256,1152]{3,2,1,0:T(8,128)(2,1)} %param.10) | copy-start | bytes 3538948
  28.2 32.8 %all-to-all-start = ((bf16[1,2,256,1152]{3,1,0,2:T(2,128)(2,1)}), bf16[1,2,256,1152]{3,1,0,2:T(2,128)(2,1)S(1)}, u32[]{:S(2)}, u32[]{:S(2)}) async-start(bf16[1,2,256,1152]{3,1,0,2:T(2,128)(2,1)} %copy.19), calls=%async_computation | async-start | bytes 2359296 | tf_op jit(solution)/shard_map/all_to_all | solution.py:195
  69.7 0.7 copy-start.1

commit v2 on v1

--- a/solution.py
+++ b/solution.py
@@ -109,42 +109,39 @@
     )(flags, q, k, v, kp, kn, vp, vn, lat, cache, wo)
 
 
-def temporal_kernel(bw_ref, q_ref, k_ref, v_ref, ind_ref, indt_ref, o_ref):
+def temporal_kernel(fid_ref, bw_ref, q_ref, k_ref, v_ref, ind_ref, indt_ref, o_ref):
     frames, tok, width = q_ref.shape
     head_dim = width // HEADS
     scaling = 1.0 / math.sqrt(head_dim)
-    bw = bw_ref[...]
+    bw = bw_ref[...].reshape(1, 1, HEADS)
     ind = ind_ref[...]
     indt = indt_ref[...]
+    fids = jnp.concatenate(
+        [jnp.full((1, 1, 1), fid_ref[g], jnp.int32) for g in range(frames)], axis=0)
 
     def body(f, carry):
         qf = q_ref[f].astype(jnp.float32)
-        scores = []
-        for g in range(frames):
-            prod = qf * k_ref[g].astype(jnp.float32)
-            s = jnp.dot(prod, ind, preferred_element_type=jnp.float32,
-                        precision=lax.Precision.HIGHEST) * scaling
-            allowed = jnp.abs(f - g) <= bw
-            scores.append(jnp.where(allowed, s, -jnp.inf))
-        top = scores[0]
-        for s in scores[1:]:
-            top = jnp.maximum(top, s)
-        expo = [jnp.exp(s - top) for s in scores]
-        total = expo[0]
-        for e in expo[1:]:
-            total = total + e
-        out = jnp.zeros((tok, width), jnp.float32)
-        for g in range(frames):
-            p = (expo[g] / total).astype(jnp.bfloat16)
-            wide = jnp.dot(p, indt, preferred_element_type=jnp.float32)
-            out = out + wide * v_ref[g].astype(jnp.float32)
+        prod = (qf[None] * k_ref[...].astype(jnp.float32)).reshape(frames * tok, width)
+        hi = prod.astype(jnp.bfloat16)
+        lo = (prod - hi.astype(jnp.float32)).astype(jnp.bfloat16)
+        s = (jnp.dot(hi, ind, preferred_element_type=jnp.float32)
+             + jnp.dot(lo, ind, preferred_element_type=jnp.float32))
+        s = s.reshape(frames, tok, HEADS) * scaling
+        allowed = jnp.abs(fids - fid_ref[f]) <= bw
+        s = jnp.where(allowed, s, -jnp.inf)
+        top = jnp.max(s, axis=0, keepdims=True)
+        expo = jnp.exp(s - top)
+        total = jnp.sum(expo, axis=0, keepdims=True)
+        p = (expo / total).astype(jnp.bfloat16).reshape(frames * tok, HEADS)
+        wide = jnp.dot(p, indt, preferred_element_type=jnp.float32).reshape(frames, tok, width)
+        out = jnp.sum(wide * v_ref[...].astype(jnp.float32), axis=0)
         o_ref[f] = out.astype(o_ref.dtype)
         return carry
 
     lax.fori_loop(0, frames, body, 0)
 
 
-def temporal_attend(packed, band_width):
+def temporal_attend(packed, band_width, fids):
     frames, tok, wide = packed.shape
     width = wide // 3
     q = packed[..., :width]
@@ -154,18 +151,44 @@
     ind = (jnp.arange(width, dtype=jnp.int32)[:, None] // head_dim
            == jnp.arange(HEADS, dtype=jnp.int32)[None, :])
     vspec = pl.BlockSpec(memory_space=pltpu.VMEM)
+    sspec = pl.BlockSpec(memory_space=pltpu.SMEM)
     cost = pl.CostEstimate(flops=frames * frames * tok * width * 40,
                            transcendentals=frames * frames * tok * HEADS,
                            bytes_accessed=2 * 4 * frames * tok * width)
     return pl.pallas_call(
         temporal_kernel,
-        in_specs=[vspec] * 6,
+        in_specs=[sspec] + [vspec] * 6,
         out_specs=vspec,
         out_shape=jax.ShapeDtypeStruct((frames, tok, width), jnp.bfloat16),
         compiler_params=pltpu.CompilerParams(vmem_limit_bytes=48 * 1024 * 1024),
         cost_estimate=cost,
-    )(band_width.reshape(1, HEADS), q, k, v, ind.astype(jnp.float32),
+    )(fids, band_width.reshape(1, HEADS), q, k, v, ind.astype(jnp.bfloat16),
       ind.T.astype(jnp.bfloat16))
+
+
+OFFSETS = ((0, 1), (-1, 0), (-1, 1), (1, 0), (1, 1), (2, 0), (2, 1))
+
+
+def frame_dest(d, dy, dc, chips):
+    return ((d // 2 + dy) % chips) * 2 + ((d % 2) ^ dc)
+
+
+def frame_perm(dy, dc, n):
+    chips = n // 2
+    return [(d, frame_dest(d, dy, dc, chips)) for d in range(n)]
+
+
+def exchange(send, n):
+    recv = {}
+    recv[(0, 1)] = lax.ppermute(send[(0, 1)], "frames", frame_perm(0, 1, n))
+    for dc in (0, 1):
+        recv[(-1, dc)] = lax.ppermute(send[(1, dc)], "frames", frame_perm(1, dc, n))
+        recv[(1, dc)] = lax.ppermute(send[(-1, dc)], "frames", frame_perm(-1, dc, n))
+    hop = lax.ppermute(send[(2, 0)], "frames", frame_perm(1, 0, n))
+    recv[(2, 0)] = lax.ppermute(hop, "frames", frame_perm(1, 0, n))
+    hop = lax.ppermute(send[(2, 1)], "frames", frame_perm(-1, 0, n))
+    recv[(2, 1)] = lax.ppermute(hop, "frames", frame_perm(-1, 1, n))
+    return recv
 
 
 def local(latent, query_rows, key_rows, value_rows, cached_out, refreshed, band_width,
@@ -191,16 +214,28 @@
                        (tile_index < total_tiles - 1).astype(jnp.int32)], axis=1)
     hidden, normed = spatial_block(flags, q, k, v, kp, kn, vp, vn, lat, cache, out_weight)
 
-    frame_groups = lax.axis_size("frames")
-    block = lax.all_to_all(normed[None], "frames", split_axis=2, concat_axis=0, tiled=True)
-    rows = block.shape[1] * block.shape[2]
+    n = lax.axis_size("frames")
+    chips = n // 2
+    chunk = tok_count // n
+    me = lax.axis_index("frames")
+    dests = {o: frame_dest(me, o[0], o[1], chips) for o in OFFSETS}
+    send = {o: lax.dynamic_slice_in_dim(normed, dests[o] * chunk, chunk, axis=1) for o in OFFSETS}
+    recv = exchange(send, n)
+    own = lax.dynamic_slice_in_dim(normed, me * chunk, chunk, axis=1)
+    block = jnp.stack([own] + [recv[o] for o in OFFSETS])
+    fids = jnp.stack([me] + [dests[o] for o in OFFSETS]).astype(jnp.int32)
+    rows = tile_count * chunk
     flat = jnp.dot(block.reshape(-1, width), temporal_weight,
                    preferred_element_type=jnp.float32).astype(jnp.bfloat16)
-    packed = flat.reshape(frame_groups, rows, 3 * width)
-    attended = temporal_attend(packed, band_width)
-    attended = attended.reshape(frame_groups, tile_count, -1, width)
-    temporal = lax.all_to_all(attended, "frames", split_axis=0, concat_axis=2, tiled=True)
-    mixed = (hidden.astype(jnp.float32) + temporal[0].astype(jnp.float32)).astype(jnp.bfloat16)
+    packed = flat.reshape(n, rows, 3 * width)
+    attended = temporal_attend(packed, band_width, fids)
+    attended = attended.reshape(n, tile_count, chunk, width)
+    back = exchange({o: attended[1 + i] for i, o in enumerate(OFFSETS)}, n)
+    temporal = lax.dynamic_update_slice_in_dim(
+        jnp.zeros_like(hidden), attended[0], me * chunk, axis=1)
+    for o in OFFSETS:
+        temporal = lax.dynamic_update_slice_in_dim(temporal, back[o], dests[o] * chunk, axis=1)
+    mixed = (hidden.astype(jnp.float32) + temporal.astype(jnp.float32)).astype(jnp.bfloat16)
     return mixed[None]
 
 

time: 115 us -> 102 us (0.89)
  blocking collectives: 19.8 us -> 0 us
  starting transfers between devices: 23.6 us -> 40.1 us
  Pallas kernels: 28.1 us -> 17 us
  waiting for transfers between devices: 27.3 us -> 30.2 us
  local copies, waits for them, and re-layouts: 4.86 us -> 2.93 us
    ppermute x0 -> x18, starting transfers between devices: none -> 32 us  [the longest x2 9.82 us: exchange(): recv[0, 1] = lax.ppermute(send[0, 1], 'frames', frame_perm(0, 1, n))]
    ppermute x0 -> x18, waiting for transfers between devices: none -> 20.4 us  [the longest x2 10.8 us: exchange(): hop = lax.ppermute(send[2, 0], 'frames', frame_perm(1, 0, n))]
    all_to_all x1 -> x0, blocking collectives: 19.8 us -> none  [local(): lax.all_to_all(attended, 'frames', split_axis=0, concat_axis=2, tiled=True)]
    all_to_all x1 -> x0, waiting for transfers between devices: 17.1 us -> none  [local(): lax.all_to_all(normed[None], 'frames', split_axis=2, concat_axis=0, tiled...]
    all_to_all x1 -> x0, starting transfers between devices: 15.5 us -> none  [local(): lax.all_to_all(normed[None], 'frames', split_axis=2, concat_axis=0, tiled...]
    pallas_call x1, Pallas kernels: 22.6 us -> 11.4 us  [temporal_attend(): pl.pallas_call(temporal_kernel, in_specs=[sspec] + [vspec] * 6, out_specs...]
    broadcast_in_dim x1, local copies, waits for them, and re-layouts: 2.23 us -> 0.09 us  [local(): jnp.zeros_like(hidden)]
  transfers between devices with their start and end apart: 3 -> 20, of which waited for: 3 -> 7; matrix products, arithmetic and copies ran while one was open for 0% -> 1% of each run, Pallas kernels for 0% -> 0%
where the time goes in v2:
time: 102 us; the launch traced here: 101 us
  starting transfers between devices  40.1 us (39%)
  waiting for transfers between devices  30.2 us (30%)
  Pallas kernels  17 us (17%)
  matrix products  8.42 us (8%)
  local copies, waits for them, and re-layouts  2.93 us (3%)
  other arithmetic  1.82 us (2%)
    pallas_call x1, Pallas kernels, temporal_attend(): pl.pallas_call(temporal_kernel, in_specs=[sspec] + [vspec] * 6, out_specs...  11.4 us
    ppermute x2, waiting for transfers between devices, exchange(): hop = lax.ppermute(send[2, 0], 'frames', frame_perm(1, 0, n))  10.8 us
    ppermute x2, starting transfers between devices, exchange(): recv[0, 1] = lax.ppermute(send[0, 1], 'frames', frame_perm(0, 1, n))  9.82 us
    ppermute x2, waiting for transfers between devices, shifted(): return lax.ppermute(block, axis, route)  9.75 us
    ppermute x2, waiting for transfers between devices, exchange(): recv[2, 0] = lax.ppermute(hop, 'frames', frame_perm(1, 0, n))  8.53 us
    dot_general x1, matrix products, local(): jnp.dot(block.reshape(-1, width), temporal_weight, preferred_element_type...  8.42 us
    ppermute x2, starting transfers between devices, shifted(): return lax.ppermute(block, axis, route)  8.13 us
    ppermute x2, starting transfers between devices, exchange(): hop = lax.ppermute(send[2, 1], 'frames', frame_perm(-1, 0, n))  5.6 us
  transfers between devices with their start and end apart: 20, of which 7 were waited for; matrix products, arithmetic and copies ran while one was open for 1% of the time, Pallas kernels for 0%

profile of v2, /device:TPU:6, one launch (start us, length us, event | category | flops | bytes accessed | tf_op | source)
XLA Modules:
  0.0 101.0 jit_solution(8644820766949016961)
XLA Ops:
  0.0 1.4 %fusion.8 = (bf16[1,64,1152]{2,1,0:T(8,128)(2,1)S(1)}, bf16[1,64,1152]{2,1,0:T(8,128)(2,1)S(1)}, bf16[1,64,1152]{2,1,0:T(8,128)(2,1)S(1)}, bf16[1,64,1152]{2,1,0...) fusion(bf16[2,256,1152]{2,1,0:T(8,128)(2,1)} %bitcast.51, ...), kind=kLoop, calls=%fused_computation.49 | loop fusion | bytes 2359296 | tf_op jit(solution)/shard_map/slice | solution.py:209
  1.5 6.2 %collective-permute-start.1 = (bf16[2,64,1152]{2,1,0:T(8,128)(2,1)S(1)}, bf16[2,64,1152]{2,1,0:T(8,128)(2,1)S(1)}, u32[]{:S(2)}, u32[]{:S(2)}) collective-permute-start(bf16[2,64,1152]{2,1,0:T(8,128)(2,1)S(1)} %pad_maximum_fusion.2), channel_id=1, source_target_pairs={{1,0},{2,1},{3,2},{4,3},{5,4},{6,5},{7,6},{8,7},{9,8},{10,9},{11,1... | collective-permute-start | bytes 884744 | tf_op jit(solution)/shard_map/ppermute | solution.py:18
  7.8 1.9 %collective-permute-start = (bf16[2,64,1152]{2,1,0:T(8,128)(2,1)S(1)}, bf16[2,64,1152]{2,1,0:T(8,128)(2,1)S(1)}, u32[]{:S(2)}, u32[]{:S(2)}) collective-permute-start(bf16[2,64,1152]{2,1,0:T(8,128)(2,1)S(1)} %pad_maximum_fusion), channel_id=1, source_target_pairs={{0,1},{1,2},{2,3},{3,4},{4,5},{5,6},{6,7},{7,8},{8,9},{9,10},{10,1... | collective-permute-start | bytes 884744 | tf_op jit(solution)/shard_map/ppermute | solution.py:18
  10.4 3.6 %collective-permute-done.1 = bf16[2,64,1152]{2,1,0:T(8,128)(2,1)S(1)} collective-permute-done((bf16[2,64,1152]{2,1,0:T(8,128)(2,1)S(1)}, bf16[2,64,1152]{2,1,0:T(8,128)(2,1)S(1)}, u32[]{:S(2)}, u32[]{:S(2)}) %collective-permute-start.1) | collective-permute-done | bytes 294944 | tf_op jit(solution)/shard_map/ppermute | solution.py:18
  14.0 6.2 %collective-permute-done = bf16[2,64,1152]{2,1,0:T(8,128)(2,1)S(1)} collective-permute-done((bf16[2,64,1152]{2,1,0:T(8,128)(2,1)S(1)}, bf16[2,64,1152]{2,1,0:T(8,128)(2,1)S(1)}, u32[]{:S(2)}, u32[]{:S(2)}) %collective-permute-start) | collective-permute-done | bytes 294944 | tf_op jit(solution)/shard_map/ppermute | solution.py:18
  20.4 5.6 %shard_map.91 = (bf16[2,256,1152]{2,1,0:T(8,128)(2,1)S(1)}, bf16[2,256,1152]{2,1,0:T(8,128)(2,1)S(1)}) custom-call(s32[2,3]{1,0:T(2,128)S(1)} %pad_add_fusion.flags_ref, bf16[2,256,1152]{2,1,0:T(8,128)(2,1)S(1)} %bitcast.48, bf16[2,256,1152]{2,1,0:T(8,128)(2,1)S(1)} %bitcast.46, bf16[2,256,1152]{2,1,0:T(8,128)(2,1)} %bitcast.52, ...), custom_call_target="tpu_custom_call" | custom-call | flops 4580179968 | bytes 10911744 | tf_op jit(solution)/shard_map/pallas_call | solution.py:95
  26.1 9.7 %collective-permute-start.2 = (bf16[2,32,1152]{2,1,0:T(8,128)(2,1)S(1)}, bf16[2,32,1152]{2,1,0:T(8,128)(2,1)S(1)}, u32[]{:S(2)}, u32[]{:S(2)}) collective-permute-start(bf16[2,32,1152]{2,1,0:T(8,128)(2,1)S(1)} %get-tuple-element.26), channel_id=1, source_target_pairs={{0,16},{16,0},{32,48},{48,32},{64,80},{80,64},{96,112},{112,96},{1... | collective-permute-start | bytes 442376 | tf_op jit(solution)/shard_map/ppermute | solution.py:183
  35.8 3.0 %collective-permute-start.3 = (bf16[2,32,1152]{2,1,0:T(8,128)(2,1)S(1)}, bf16[2,32,1152]{2,1,0:T(8,128)(2,1)S(1)}, u32[]{:S(2)}, u32[]{:S(2)}) collective-permute-start(bf16[2,32,1152]{2,1,0:T(8,128)(2,1)S(1)} %get-tuple-element.25), channel_id=1, source_target_pairs={{0,32},{16,48},{32,64},{48,80},{64,96},{80,112},{96,0},{112,16},{1... | collective-permute-start | bytes 442376 | tf_op jit(solution)/shard_map/ppermute | solution.py:185
  38.8 3.0 %collective-permute-start.5 = (bf16[2,32,1152]{2,1,0:T(8,128)(2,1)S(1)}, bf16[2,32,1152]{2,1,0:T(8,128)(2,1)S(1)}, u32[]{:S(2)}, u32[]{:S(2)}) collective-permute-start(bf16[2,32,1152]{2,1,0:T(8,128)(2,1)S(1)} %get-tuple-element.23), channel_id=1, source_target_pairs={{0,96},{16,112},{32,0},{48,16},{64,32},{80,48},{96,64},{112,80},{1... | collective-permute-start | bytes 442376 | tf_op jit(solution)/shard_map/ppermute | solution.py:186
  41.8 3.3 %collective-permute-start.9 = (bf16[2,32,1152]{2,1,0:T(8,128)(2,1)S(1)}, bf16[2,32,1152]{2,1,0:T(8,128)(2,1)S(1)}, u32[]{:S(2)}, u32[]{:S(2)}) collective-permute-start(bf16[2,32,1152]{2,1,0:T(8,128)(2,1)S(1)} %get-tuple-element.20), channel_id=1, source_target_pairs={{0,96},{16,112},{32,0},{48,16},{64,32},{80,48},{96,64},{112,80},{1... | collective-permute-start | bytes 442376 | tf_op jit(solution)/shard_map/ppermute | solution.py:189
  45.6 5.4 %collective-permute-done.7 = bf16[2,32,1152]{2,1,0:T(8,128)(2,1)S(1)} collective-permute-done((bf16[2,32,1152]{2,1,0:T(8,128)(2,1)S(1)}, bf16[2,32,1152]{2,1,0:T(8,128)(2,1)S(1)}, u32[]{:S(2)}, u32[]{:S(2)}) %collective-permute-start.7) | collective-permute-done | bytes 147488 | tf_op jit(solution)/shard_map/ppermute | solution.py:187
  51.3 2.1 %collective-permute-start.10 = (bf16[2,32,1152]{2,1,0:T(8,128)(2,1)S(1)}, bf16[2,32,1152]{2,1,0:T(8,128)(2,1)S(1)}, u32[]{:S(2)}, u32[]{:S(2)}) collective-permute-start(bf16[2,32,1152]{2,1,0:T(8,128)(2,1)S(1)} %collective-permute-done.9), channel_id=1, source_target_pairs={{0,112},{16,96},{32,16},{48,0},{64,48},{80,32},{96,80},{112,64},{1... | collective-permute-start | bytes 442376 | tf_op jit(solution)/shard_map/ppermute | solution.py:190
  53.5 4.3 %collective-permute-done.8 = bf16[2,32,1152]{2,1,0:T(8,128)(2,1)S(1)} collective-permute-done((bf16[2,32,1152]{2,1,0:T(8,128)(2,1)S(1)}, bf16[2,32,1152]{2,1,0:T(8,128)(2,1)S(1)}, u32[]{:S(2)}, u32[]{:S(2)}) %collective-permute-start.8) | collective-permute-done | bytes 147488 | tf_op jit(solution)/shard_map/ppermute | solution.py:188
  57.8 8.4 %convolution_convert_fusion = bf16[512,3456]{1,0:T(8,128)(2,1)S(1)} fusion(bf16[512,1152]{1,0:T(8,128)(2,1)S(1)} %bitcast.60, bf16[1152,3456]{1,0:T(8,128)(2,1)} %param.17), kind=kOutput, calls=%fused_computation | convolution fusion | flops 4078632960 | bytes 12681216 | tf_op jit(solution)/shard_map/dot_general | solution.py:228
  66.9 11.4 %shard_map.92 = bf16[8,64,1152]{2,1,0:T(8,128)(2,1)S(1)} custom-call(s32[8]{0:T(128)S(1)} %stack.76.fid_ref, s32[1,16]{1,0:T(1,128)S(1)} %bitcast.47, bf16[8,64,1152]{2,1,0:T(8,128)(2,1)S(1)} %get-tuple-element.11.q_ref, bf16[8,64,1152]{2,1,0:T(8,128)(2,1)S(1)} %get-tuple-element.10.k_ref, bf16[8,64,1152]{2,1,0:T(8,128)(2,1)S(1)} %get-tuple-element.9.v_ref, ...), custom_call_target="tpu_custom_call" | custom-call | flops 188743680 | bytes 4718592 | tf_op jit(solution)/shard_map/pallas_call | solution.py:158
  78.6 2.2 %collective-permute-start.13 = (bf16[2,32,1152]{2,1,0:T(8,128)(2,1)S(1)}, bf16[2,32,1152]{2,1,0:T(8,128)(2,1)S(1)}, u32[]{:S(2)}, u32[]{:S(2)}) collective-permute-start(bf16[2,32,1152]{2,1,0:T(8,128)(2,1)S(1)} %bitcast.55), channel_id=1, source_target_pairs={{0,48},{16,32},{32,80},{48,64},{64,112},{80,96},{96,16},{112,0},{1... | collective-permute-start | bytes 442376 | tf_op jit(solution)/shard_map/ppermute | solution.py:185
  80.8 1.5 %collective-permute-start.14 = (bf16[2,32,1152]{2,1,0:T(8,128)(2,1)S(1)}, bf16[2,32,1152]{2,1,0:T(8,128)(2,1)S(1)}, u32[]{:S(2)}, u32[]{:S(2)}) collective-permute-start(bf16[2,32,1152]{2,1,0:T(8,128)(2,1)S(1)} %bitcast.54), channel_id=1, source_target_pairs={{0,96},{16,112},{32,0},{48,16},{64,32},{80,48},{96,64},{112,80},{1... | collective-permute-start | bytes 442376 | tf_op jit(solution)/shard_map/ppermute | solution.py:186
  82.2 1.0 %collective-permute-start.16 = (bf16[2,32,1152]{2,1,0:T(8,128)(2,1)S(1)}, bf16[2,32,1152]{2,1,0:T(8,128)(2,1)S(1)}, u32[]{:S(2)}, u32[]{:S(2)}) collective-permute-start(bf16[2,32,1152]{2,1,0:T(8,128)(2,1)S(1)} %bitcast.57), channel_id=1, source_target_pairs={{0,32},{16,48},{32,64},{48,80},{64,96},{80,112},{96,0},{112,16},{1... | collective-permute-start | bytes 442376 | tf_op jit(solution)/shard_map/ppermute | solution.py:187
  83.4 2.3 %collective-permute-start.18 = (bf16[2,32,1152]{2,1,0:T(8,128)(2,1)S(1)}, bf16[2,32,1152]{2,1,0:T(8,128)(2,1)S(1)}, u32[]{:S(2)}, u32[]{:S(2)}) collective-permute-start(bf16[2,32,1152]{2,1,0:T(8,128)(2,1)S(1)} %bitcast.56), channel_id=1, source_target_pairs={{0,96},{16,112},{32,0},{48,16},{64,32},{80,48},{96,64},{112,80},{1... | collective-permute-start | bytes 442376 | tf_op jit(solution)/shard_map/ppermute | solution.py:189
  85.7 1.1 %collective-permute-done.12 = bf16[2,32,1152]{2,1,0:T(8,128)(2,1)S(1)} collective-permute-done((bf16[2,32,1152]{2,1,0:T(8,128)(2,1)S(1)}, bf16[2,32,1152]{2,1,0:T(8,128)(2,1)S(1)}, u32[]{:S(2)}, u32[]{:S(2)}) %collective-permute-start.12) | collective-permute-done | bytes 147488 | tf_op jit(solution)/shard_map/ppermute | solution.py:185
  87.4 5.4 %collective-permute-done.16 = bf16[2,32,1152]{2,1,0:T(8,128)(2,1)S(1)} collective-permute-done((bf16[2,32,1152]{2,1,0:T(8,128)(2,1)S(1)}, bf16[2,32,1152]{2,1,0:T(8,128)(2,1)S(1)}, u32[]{:S(2)}, u32[]{:S(2)}) %collective-permute-start.16) | collective-permute-done | bytes 147488 | tf_op jit(solution)/shard_map/ppermute | solution.py:187
  92.8 2.4 %collective-permute-start.19 = (bf16[2,32,1152]{2,1,0:T(8,128)(2,1)S(1)}, bf16[2,32,1152]{2,1,0:T(8,128)(2,1)S(1)}, u32[]{:S(2)}, u32[]{:S(2)}) collective-permute-start(bf16[2,32,1152]{2,1,0:T(8,128)(2,1)S(1)} %collective-permute-done.18), channel_id=1, source_target_pairs={{0,112},{16,96},{32,16},{48,0},{64,48},{80,32},{96,80},{112,64},{1... | collective-permute-start | bytes 442376 | tf_op jit(solution)/shard_map/ppermute | solution.py:190
  95.4 4.3 %collective-permute-done.17 = bf16[2,32,1152]{2,1,0:T(8,128)(2,1)S(1)} collective-permute-done((bf16[2,32,1152]{2,1,0:T(8,128)(2,1)S(1)}, bf16[2,32,1152]{2,1,0:T(8,128)(2,1)S(1)}, u32[]{:S(2)}, u32[]{:S(2)}) %collective-permute-start.17) | collective-permute-done | bytes 147488 | tf_op jit(solution)/shard_map/ppermute | solution.py:188
  99.7 1.3 %fusion = bf16[1,2,256,1152]{3,2,1,0:T(8,128)(2,1)} fusion(bf16[2,256,1152]{2,1,0:T(8,128)(2,1)S(1)} %constant_dynamic-update-slice_fusion, bf16[2,256,1152]{2,1,0:T(8,128)(2,1)S(1)} %get-tuple-element.7), kind=kLoop, calls=%fused_computation.2 | loop fusion | flops 2359296 | bytes 3538944 | tf_op jit(solution)/shard_map/broadcast_in_dim | solution.py:239
  (64 shorter events, 3.7 us)
Async XLA Ops:
  1.4 8.4 %copy-start.3 = (s32[1,2]{1,0:T(1,128)S(1)}, s32[1,2]{1,0:T(1,128)}, u32[]{:S(2)}) copy-start(s32[1,2]{1,0:T(1,128)} %param.14) | copy-start | bytes 28
  1.5 12.5 %collective-permute-start.1 = (bf16[2,64,1152]{2,1,0:T(8,128)(2,1)S(1)}, bf16[2,64,1152]{2,1,0:T(8,128)(2,1)S(1)}, u32[]{:S(2)}, u32[]{:S(2)}) collective-permute-start(bf16[2,64,1152]{2,1,0:T(8,128)(2,1)S(1)} %pad_maximum_fusion.2), channel_id=1, source_target_pairs={{1,0},{2,1},{3,2},{4,3},{5,4},{6,5},{7,6},{8,7},{9,8},{10,9},{11,1... | collective-permute-start | bytes 884744 | tf_op jit(solution)/shard_map/ppermute | solution.py:18
  7.8 12.5 %collective-permute-start = (bf16[2,64,1152]{2,1,0:T(8,128)(2,1)S(1)}, bf16[2,64,1152]{2,1,0:T(8,128)(2,1)S(1)}, u32[]{:S(2)}, u32[]{:S(2)}) collective-permute-start(bf16[2,64,1152]{2,1,0:T(8,128)(2,1)S(1)} %pad_maximum_fusion), channel_id=1, source_target_pairs={{0,1},{1,2},{2,3},{3,4},{4,5},{5,6},{6,7},{7,8},{8,9},{9,10},{10,1... | collective-permute-start | bytes 884744 | tf_op jit(solution)/shard_map/ppermute | solution.py:18
  14.0 6.4 %copy-start = (bf16[1,2,256,1152]{3,2,1,0:T(8,128)(2,1)S(1)}, bf16[1,2,256,1152]{3,2,1,0:T(8,128)(2,1)}, u32[]{:S(2)}) copy-start(bf16[1,2,256,1152]{3,2,1,0:T(8,128)(2,1)} %param.11) | copy-start | bytes 3538948
  14.0 6.4 %copy-start.2 = (bf16[1,2,256,1152]{3,2,1,0:T(8,128)(2,1)S(1)}, bf16[1,2,256,1152]{3,2,1,0:T(8,128)(2,1)}, u32[]{:S(2)}) copy-start(bf16[1,2,256,1152]{3,2,1,0:T(8,128)(2,1)} %param.10) | copy-start | bytes 3538948
  26.1 15.7 %collective-permute-start.2 = (bf16[2,32,1152]{2,1,0:T(8,128)(2,1)S(1)}, bf16[2,32,1152]{2,1,0:T(8,128)(2,1)S(1)}, u32[]{:S(2)}, u32[]{:S(2)}) collective-permute-start(bf16[2,32,1152]{2,1,0:T(8,128)(2,1)S(1)} %get-tuple-element.26), channel_id=1, source_target_pairs={{0,16},{16,0},{32,48},{48,32},{64,80},{80,64},{96,112},{112,96},{1... | collective-permute-start | bytes 442376 | tf_op jit(solution)/shard_map/ppermute | solution.py:183
  35.8 9.3 %collective-permute-start.3 = (bf16[2,32,1152]{2,1,0:T(8,128)(2,1)S(1)}, bf16[2,32,1152]{2,1,0:T(8,128)(2,1)S(1)}, u32[]{:S(2)}, u32[]{:S(2)}) collective-permute-start(bf16[2,32,1152]{2,1,0:T(8,128)(2,1)S(1)} %get-tuple-element.25), channel_id=1, source_target_pairs={{0,32},{16,48},{32,64},{48,80},{64,96},{80,112},{96,0},{112,16},{1... | collective-permute-start | bytes 442376 | tf_op jit(solution)/shard_map/ppermute | solution.py:185
  38.8 14.6 %collective-permute-start.4 = (bf16[2,32,1152]{2,1,0:T(8,128)(2,1)S(1)}, bf16[2,32,1152]{2,1,0:T(8,128)(2,1)S(1)}, u32[]{:S(2)}, u32[]{:S(2)}) collective-permute-start(bf16[2,32,1152]{2,1,0:T(8,128)(2,1)S(1)} %get-tuple-element.24), channel_id=1, source_target_pairs={{0,48},{16,32},{32,80},{48,64},{64,112},{80,96},{96,16},{112,0},{1... | collective-permute-start | bytes 442376 | tf_op jit(solution)/shard_map/ppermute | solution.py:185
  38.8 14.6 %collective-permute-start.5 = (bf16[2,32,1152]{2,1,0:T(8,128)(2,1)S(1)}, bf16[2,32,1152]{2,1,0:T(8,128)(2,1)S(1)}, u32[]{:S(2)}, u32[]{:S(2)}) collective-permute-start(bf16[2,32,1152]{2,1,0:T(8,128)(2,1)S(1)} %get-tuple-element.23), channel_id=1, source_target_pairs={{0,96},{16,112},{32,0},{48,16},{64,32},{80,48},{96,64},{112,80},{1... | collective-permute-start | bytes 442376 | tf_op jit(solution)/shard_map/ppermute | solution.py:186
  41.8 9.2 %collective-permute-start.7 = (bf16[2,32,1152]{2,1,0:T(8,128)(2,1)S(1)}, bf16[2,32,1152]{2,1,0:T(8,128)(2,1)S(1)}, u32[]{:S(2)}, u32[]{:S(2)}) collective-permute-start(bf16[2,32,1152]{2,1,0:T(8,128)(2,1)S(1)} %get-tuple-element.21), channel_id=1, source_target_pairs={{0,32},{16,48},{32,64},{48,80},{64,96},{80,112},{96,0},{112,16},{1... | collective-permute-start | bytes 442376 | tf_op jit(solution)/shard_map/ppermute | solution.py:187
  41.8 9.5 %collective-permute-start.9 = (bf16[2,32,1152]{2,1,0:T(8,128)(2,1)S(1)}, bf16[2,32,1152]{2,1,0:T(8,128)(2,1)S(1)}, u32[]{:S(2)}, u32[]{:S(2)}) collective-permute-start(bf16[2,32,1152]{2,1,0:T(8,128)(2,1)S(1)} %get-tuple-element.20), channel_id=1, source_target_pairs={{0,96},{16,112},{32,0},{48,16},{64,32},{80,48},{96,64},{112,80},{1... | collective-permute-start | bytes 442376 | tf_op jit(solution)/shard_map/ppermute | solution.py:189
  45.1 8.3 %collective-permute-start.6 = (bf16[2,32,1152]{2,1,0:T(8,128)(2,1)S(1)}, bf16[2,32,1152]{2,1,0:T(8,128)(2,1)S(1)}, u32[]{:S(2)}, u32[]{:S(2)}) collective-permute-start(bf16[2,32,1152]{2,1,0:T(8,128)(2,1)S(1)} %get-tuple-element.22), channel_id=1, source_target_pairs={{0,112},{16,96},{32,16},{48,0},{64,48},{80,32},{96,80},{112,64},{1... | collective-permute-start | bytes 442376 | tf_op jit(solution)/shard_map/ppermute | solution.py:186
  51.0 6.8 %collective-permute-start.8 = (bf16[2,32,1152]{2,1,0:T(8,128)(2,1)S(1)}, bf16[2,32,1152]{2,1,0:T(8,128)(2,1)S(1)}, u32[]{:S(2)}, u32[]{:S(2)}) collective-permute-start(bf16[2,32,1152]{2,1,0:T(8,128)(2,1)S(1)} %collective-permute-done.7), channel_id=1, source_target_pairs={{0,32},{16,48},{32,64},{48,80},{64,96},{80,112},{96,0},{112,16},{1... | collective-permute-start | bytes 442376 | tf_op jit(solution)/shard_map/ppermute | solution.py:188
  51.3 6.5 %collective-permute-start.10 = (bf16[2,32,1152]{2,1,0:T(8,128)(2,1)S(1)}, bf16[2,32,1152]{2,1,0:T(8,128)(2,1)S(1)}, u32[]{:S(2)}, u32[]{:S(2)}) collective-permute-start(bf16[2,32,1152]{2,1,0:T(8,128)(2,1)S(1)} %collective-permute-done.9), channel_id=1, source_target_pairs={{0,112},{16,96},{32,16},{48,0},{64,48},{80,32},{96,80},{112,64},{1... | collective-permute-start | bytes 442376 | tf_op jit(solution)/shard_map/ppermute | solution.py:190
  66.3 0.7 copy-start.1
  78.4 5.0 %collective-permute-start.11 = (bf16[2,32,1152]{2,1,0:T(8,128)(2,1)S(1)}, bf16[2,32,1152]{2,1,0:T(8,128)(2,1)S(1)}, u32[]{:S(2)}, u32[]{:S(2)}) collective-permute-start(bf16[2,32,1152]{2,1,0:T(8,128)(2,1)S(1)} %bitcast.59), channel_id=1, source_target_pairs={{0,16},{16,0},{32,48},{48,32},{64,80},{80,64},{96,112},{112,96},{1... | collective-permute-start | bytes 442376 | tf_op jit(solution)/shard_map/ppermute | solution.py:183
  78.5 8.3 %collective-permute-start.12 = (bf16[2,32,1152]{2,1,0:T(8,128)(2,1)S(1)}, bf16[2,32,1152]{2,1,0:T(8,128)(2,1)S(1)}, u32[]{:S(2)}, u32[]{:S(2)}) collective-permute-start(bf16[2,32,1152]{2,1,0:T(8,128)(2,1)S(1)} %bitcast.58), channel_id=1, source_target_pairs={{0,32},{16,48},{32,64},{48,80},{64,96},{80,112},{96,0},{112,16},{1... | collective-permute-start | bytes 442376 | tf_op jit(solution)/shard_map/ppermute | solution.py:185
  78.6 16.7 %collective-permute-start.13 = (bf16[2,32,1152]{2,1,0:T(8,128)(2,1)S(1)}, bf16[2,32,1152]{2,1,0:T(8,128)(2,1)S(1)}, u32[]{:S(2)}, u32[]{:S(2)}) collective-permute-start(bf16[2,32,1152]{2,1,0:T(8,128)(2,1)S(1)} %bitcast.55), channel_id=1, source_target_pairs={{0,48},{16,32},{32,80},{48,64},{64,112},{80,96},{96,16},{112,0},{1... | collective-permute-start | bytes 442376 | tf_op jit(solution)/shard_map/ppermute | solution.py:185
  80.8 14.6 %collective-permute-start.14 = (bf16[2,32,1152]{2,1,0:T(8,128)(2,1)S(1)}, bf16[2,32,1152]{2,1,0:T(8,128)(2,1)S(1)}, u32[]{:S(2)}, u32[]{:S(2)}) collective-permute-start(bf16[2,32,1152]{2,1,0:T(8,128)(2,1)S(1)} %bitcast.54), channel_id=1, source_target_pairs={{0,96},{16,112},{32,0},{48,16},{64,32},{80,48},{96,64},{112,80},{1... | collective-permute-start | bytes 442376 | tf_op jit(solution)/shard_map/ppermute | solution.py:186
  82.2 10.6 %collective-permute-start.16 = (bf16[2,32,1152]{2,1,0:T(8,128)(2,1)S(1)}, bf16[2,32,1152]{2,1,0:T(8,128)(2,1)S(1)}, u32[]{:S(2)}, u32[]{:S(2)}) collective-permute-start(bf16[2,32,1152]{2,1,0:T(8,128)(2,1)S(1)} %bitcast.57), channel_id=1, source_target_pairs={{0,32},{16,48},{32,64},{48,80},{64,96},{80,112},{96,0},{112,16},{1... | collective-permute-start | bytes 442376 | tf_op jit(solution)/shard_map/ppermute | solution.py:187
  83.4 9.5 %collective-permute-start.18 = (bf16[2,32,1152]{2,1,0:T(8,128)(2,1)S(1)}, bf16[2,32,1152]{2,1,0:T(8,128)(2,1)S(1)}, u32[]{:S(2)}, u32[]{:S(2)}) collective-permute-start(bf16[2,32,1152]{2,1,0:T(8,128)(2,1)S(1)} %bitcast.56), channel_id=1, source_target_pairs={{0,96},{16,112},{32,0},{48,16},{64,32},{80,48},{96,64},{112,80},{1... | collective-permute-start | bytes 442376 | tf_op jit(solution)/shard_map/ppermute | solution.py:189
  86.8 8.6 %collective-permute-start.15 = (bf16[2,32,1152]{2,1,0:T(8,128)(2,1)S(1)}, bf16[2,32,1152]{2,1,0:T(8,128)(2,1)S(1)}, u32[]{:S(2)}, u32[]{:S(2)}) collective-permute-start(bf16[2,32,1152]{2,1,0:T(8,128)(2,1)S(1)} %bitcast.53), channel_id=1, source_target_pairs={{0,112},{16,96},{32,16},{48,0},{64,48},{80,32},{96,80},{112,64},{1... | collective-permute-start | bytes 442376 | tf_op jit(solution)/shard_map/ppermute | solution.py:186
  92.8 6.8 %collective-permute-start.17 = (bf16[2,32,1152]{2,1,0:T(8,128)(2,1)S(1)}, bf16[2,32,1152]{2,1,0:T(8,128)(2,1)S(1)}, u32[]{:S(2)}, u32[]{:S(2)}) collective-permute-start(bf16[2,32,1152]{2,1,0:T(8,128)(2,1)S(1)} %collective-permute-done.16), channel_id=1, source_target_pairs={{0,32},{16,48},{32,64},{48,80},{64,96},{80,112},{96,0},{112,16},{1... | collective-permute-start | bytes 442376 | tf_op jit(solution)/shard_map/ppermute | solution.py:188
  92.8 6.8 %collective-permute-start.19 = (bf16[2,32,1152]{2,1,0:T(8,128)(2,1)S(1)}, bf16[2,32,1152]{2,1,0:T(8,128)(2,1)S(1)}, u32[]{:S(2)}, u32[]{:S(2)}) collective-permute-start(bf16[2,32,1152]{2,1,0:T(8,128)(2,1)S(1)} %collective-permute-done.18), channel_id=1, source_target_pairs={{0,112},{16,96},{32,16},{48,0},{64,48},{80,32},{96,80},{112,64},{1... | collective-permute-start | bytes 442376 | tf_op jit(solution)/shard_map/ppermute | solution.py:190
